TPU v7x, 512 devices: a whole 4x4x16 slice. The times are simulated.
512 devices in a mesh: req: 128 (over z, x, core), head: 4 (over y).
Axes of the slice: x: 4, y: 4, z: 16, core: 2. Of those that a mesh axis runs over, the one named last changes fastest.
Arguments:
- query_proj: bfloat16 [32768, 2048], P('req', 'head'), may hold values from -6 to 6
- key_proj: bfloat16 [32768, 2048], P('req', 'head'), may hold values from -6 to 6
- value_proj: bfloat16 [32768, 2048], P('req', 'head'), may hold values from -6 to 6
- lengths: int32 [64], replicated, may hold values from 1 to 8, 256 in all
- page_table: int32 [256], P('req'), may hold values from 0 to 255, as said below
- out_weight: bfloat16 [2048, 4096], P('req', 'head'), may hold values from -0.125 to 0.125
- out_bias: float32 [4096], P('head'), may hold values from -3 to 3
Outputs:
- attended: bfloat16 [32768, 4096], P('req', 'head')
- kv_pages: bfloat16 [256, 2, 128, 2048], P('req', None, None, 'head')
Inputs may be any that keep to these rules, and one draw needn't show every extreme that they name: page_table is a permutation in which page b of the stream goes to one of the pages 2 * (b // 2) to 2 * (b // 2) + 1.
All inputs are finite; a program needn't handle non-finite values.
Results may differ from a plain program's by a relative error of at most 0.0046.
Values may be sent and summed in bfloat16 or wider, within the bound.
No kernel may reach another device: no remote copies, remote signals or barrier semaphores. Data moves between devices by JAX's collectives and lax.ppermute only.
A program may use at most 64 MiB of HBM per device.

v0:
```python
import math
import jax
import jax.numpy as jnp
from jax import lax
from jax.sharding import Mesh, PartitionSpec as P

DH = 128
ROT = 32
PAGE = 128
BLK_DEV = 2
REACH = 4
TOK_DEV = 256
rope_base = 10000.0
REQ = ("z", "x", "core")


def passed_along(array, axis, by):
    count = lax.axis_size(axis)
    pairs = [(i, i + by) for i in range(count) if 0 <= i + by < count]
    return lax.ppermute(array, axis, pairs)


def request_info(lengths, token_index):
    request_ends = jnp.cumsum(lengths) * PAGE
    request_starts = request_ends - lengths * PAGE
    inside = request_starts[None, :] <= token_index[:, None]
    request_id = jnp.sum(inside.astype(jnp.int32), axis=1) - 1
    opening = jnp.max(jnp.where(inside, request_starts[None, :], 0), axis=1)
    return (request_id, token_index - opening)


def rotate_heads(projected, position):
    values_f32 = projected.astype(jnp.float32)
    half_rot = ROT // 2
    frequency = jnp.exp(
        jnp.arange(half_rot, dtype=jnp.float32) * (-2.0 * math.log(rope_base) / ROT)
    )
    angles = position.astype(jnp.float32)[:, None] * frequency[None, :]
    cosine = jnp.cos(angles)[:, None, :]
    sine = jnp.sin(angles)[:, None, :]
    front_half = values_f32[..., :half_rot]
    back_half = values_f32[..., half_rot:ROT]
    turned = jnp.concatenate(
        [
            front_half * cosine - back_half * sine,
            back_half * cosine + front_half * sine,
            values_f32[..., ROT:],
        ],
        axis=-1,
    )
    return turned.astype(jnp.bfloat16)


def attend_block(query_rot, key_rot, value_rows, query_id, query_token, key_id, key_token):
    scores = jnp.einsum("qhd,khd->hqk", query_rot, key_rot, preferred_element_type=jnp.float32) * (
        1.0 / math.sqrt(DH)
    )
    allowed = (query_id[:, None] == key_id[None, :]) & (key_token[None, :] <= query_token[:, None])
    scores = jnp.where(allowed[None], scores, -jnp.inf)
    row_max = jnp.max(scores, axis=-1, keepdims=True)
    raised = jnp.exp(scores - row_max)
    probs = (raised / jnp.sum(raised, axis=-1, keepdims=True)).astype(jnp.bfloat16)
    mixed = jnp.einsum("hqk,khd->qhd", probs, value_rows, preferred_element_type=jnp.float32)
    return mixed.astype(jnp.bfloat16)


def local(query_proj, key_proj, value_proj, lengths, page_table, out_weight, out_bias):
    local_heads = query_proj.shape[1] // DH
    device_rank = lax.axis_index(REQ)
    first_token = device_rank * TOK_DEV
    own_tokens = first_token + jnp.arange(TOK_DEV, dtype=jnp.int32)
    request_id, position = request_info(lengths, own_tokens)
    query_rot = rotate_heads(query_proj.reshape(TOK_DEV, local_heads, DH), position)
    key_flat = rotate_heads(key_proj.reshape(TOK_DEV, local_heads, DH), position).reshape(
        TOK_DEV, local_heads * DH
    )
    key_list = [key_flat]
    value_list = [value_proj]
    for distance in range(1, REACH + 1):
        far_key, far_value = passed_along((key_flat, value_proj), REQ, distance)
        key_list.append(far_key)
        value_list.append(far_value)
    key_stack = jnp.stack(key_list[::-1], axis=0)
    value_stack = jnp.stack(value_list[::-1], axis=0)
    key_rows = (REACH + 1) * TOK_DEV
    key_all = key_stack.reshape(key_rows, local_heads, DH)
    value_all = value_stack.reshape(key_rows, local_heads, DH)
    key_tokens = first_token - REACH * TOK_DEV + jnp.arange(key_rows, dtype=jnp.int32)
    key_id, key_position = request_info(lengths, key_tokens)
    mixed = attend_block(query_rot, key_all, value_all, request_id, own_tokens, key_id, key_tokens)
    heads_out = mixed.reshape(TOK_DEV, local_heads * DH)
    weight_rows = lax.all_gather(out_weight, "core", axis=0, tiled=True)
    weight_rows = lax.all_gather(weight_rows, "x", axis=0, tiled=True)
    weight_rows = lax.all_gather(weight_rows, "z", axis=0, tiled=True)
    heads_all = lax.all_gather(heads_out, "head", axis=1, tiled=True)
    summed = jnp.dot(heads_all, weight_rows, preferred_element_type=jnp.float32)
    attended = (summed + out_bias).astype(jnp.bfloat16)
    local_page = page_table - device_rank * BLK_DEV
    picker = (local_page[:, None] == jnp.arange(BLK_DEV, dtype=jnp.int32)[None, :]).astype(
        jnp.bfloat16
    )
    page_blocks = jnp.stack(
        [
            key_flat.reshape(BLK_DEV, PAGE, local_heads * DH),
            value_proj.reshape(BLK_DEV, PAGE, local_heads * DH),
        ],
        axis=1,
    )
    kv_pages = jnp.einsum(
        "bp,bctd->pctd", picker, page_blocks, preferred_element_type=jnp.float32
    ).astype(jnp.bfloat16)
    return (attended, kv_pages)


def solution(mesh):
    devices = mesh.devices
    cores = len({d.core_on_chip for d in devices.flat})
    columns = len({d.coords[0] for d in devices.flat})
    req_size, head_size = devices.shape
    split = Mesh(
        devices.reshape(req_size // (columns * cores), columns, cores, head_size),
        ("z", "x", "core", "head"),
    )
    placed = (
        P(REQ, "head"),
        P(REQ, "head"),
        P(REQ, "head"),
        P(),
        P(REQ),
        P(REQ, "head"),
        P("head"),
    )
    return jax.shard_map(
        local,
        mesh=split,
        in_specs=placed,
        out_specs=(P(REQ, "head"), P(REQ, None, None, "head")),
        check_vma=False,
    )
```

profile of v0, /device:TPU:2, one launch (start us, length us, event | category | flops | bytes accessed | tf_op | source)
XLA Modules:
  0.0 200.4 jit_solution(546849596047994481)
XLA Ops:
  7.2 1.1 copy.50
  8.4 0.7 copy.44
  10.7 4.0 %collective-permute-start.4 = (bf16[256,512]{0,1:T(8,128)(2,1)S(1)}, bf16[256,512]{0,1:T(8,128)(2,1)S(1)}, u32[]{:S(2)}, u32[]{:S(2)}) collective-permute-start(bf16[256,512]{0,1:T(8,128)(2,1)S(1)} %bitcast.39), channel_id=1, source_target_pairs={{0,16},{4,20},{8,24},{12,28},{16,32},{20,36},{24,40},{28,44},{32,4... | collective-permute-start | bytes 786440 | tf_op jit(solution)/shard_map/ppermute | solution.py:20
  14.7 3.0 %collective-permute-start.5 = (bf16[256,512]{0,1:T(8,128)(2,1)S(1)}, bf16[256,512]{0,1:T(8,128)(2,1)}, u32[]{:S(2)}, u32[]{:S(2)}) collective-permute-start(bf16[256,512]{0,1:T(8,128)(2,1)S(1)} %bitcast.40), channel_id=1, source_target_pairs={{0,12},{4,16},{8,20},{12,24},{16,28},{20,32},{24,36},{28,40},{32,4... | collective-permute-start | bytes 786440 | tf_op jit(solution)/shard_map/ppermute | solution.py:20
  17.7 3.3 %collective-permute-start.6 = (bf16[256,512]{0,1:T(8,128)(2,1)S(1)}, bf16[256,512]{0,1:T(8,128)(2,1)}, u32[]{:S(2)}, u32[]{:S(2)}) collective-permute-start(bf16[256,512]{0,1:T(8,128)(2,1)S(1)} %bitcast.41), channel_id=1, source_target_pairs={{0,8},{4,12},{8,16},{12,20},{16,24},{20,28},{24,32},{28,36},{32,40... | collective-permute-start | bytes 786440 | tf_op jit(solution)/shard_map/ppermute | solution.py:20
  21.0 3.5 %collective-permute-start.7 = (bf16[256,512]{0,1:T(8,128)(2,1)S(1)}, bf16[256,512]{0,1:T(8,128)(2,1)}, u32[]{:S(2)}, u32[]{:S(2)}) collective-permute-start(bf16[256,512]{0,1:T(8,128)(2,1)S(1)} %bitcast.42), channel_id=1, source_target_pairs={{0,4},{4,8},{8,12},{12,16},{16,20},{20,24},{24,28},{28,32},{32,36}... | collective-permute-start | bytes 786440 | tf_op jit(solution)/shard_map/ppermute | solution.py:20
  24.6 4.4 %collective-permute-start = (bf16[256,512]{1,0:T(8,128)(2,1)S(1)}, bf16[256,512]{1,0:T(8,128)(2,1)S(1)}, u32[]{:S(2)}, u32[]{:S(2)}) collective-permute-start(bf16[256,512]{1,0:T(8,128)(2,1)S(1)} %copy-done.2), channel_id=1, source_target_pairs={{0,16},{4,20},{8,24},{12,28},{16,32},{20,36},{24,40},{28,44},{32,4... | collective-permute-start | bytes 786440 | tf_op jit(solution)/shard_map/ppermute | solution.py:20
  30.2 1.0 pad_maximum_fusion.2
  31.2 2.1 %collective-permute-start.1 = (bf16[256,512]{1,0:T(8,128)(2,1)S(1)}, bf16[256,512]{1,0:T(8,128)(2,1)S(1)}, u32[]{:S(2)}, u32[]{:S(2)}) collective-permute-start(bf16[256,512]{1,0:T(8,128)(2,1)S(1)} %copy-done.2), channel_id=1, source_target_pairs={{0,12},{4,16},{8,20},{12,24},{16,28},{20,32},{24,36},{28,40},{32,4... | collective-permute-start | bytes 786440 | tf_op jit(solution)/shard_map/ppermute | solution.py:20
  33.3 0.7 bitcast_dynamic-update-slice_fusion.3
  34.0 0.6 collective-permute-done
  34.7 9.2 %collective-permute-start.2 = (bf16[256,512]{1,0:T(8,128)(2,1)S(1)}, bf16[256,512]{1,0:T(8,128)(2,1)}, u32[]{:S(2)}, u32[]{:S(2)}) collective-permute-start(bf16[256,512]{1,0:T(8,128)(2,1)S(1)} %copy-done.2), channel_id=1, source_target_pairs={{0,8},{4,12},{8,16},{12,20},{16,24},{20,28},{24,32},{28,36},{32,40... | collective-permute-start | bytes 786440 | tf_op jit(solution)/shard_map/ppermute | solution.py:20
  43.9 4.4 %collective-permute-start.3 = (bf16[256,512]{1,0:T(8,128)(2,1)S(1)}, bf16[256,512]{1,0:T(8,128)(2,1)}, u32[]{:S(2)}, u32[]{:S(2)}) collective-permute-start(bf16[256,512]{1,0:T(8,128)(2,1)S(1)} %copy-done.2), channel_id=1, source_target_pairs={{0,4},{4,8},{8,12},{12,16},{16,20},{20,24},{24,28},{28,32},{32,36}... | collective-permute-start | bytes 786440 | tf_op jit(solution)/shard_map/ppermute | solution.py:20
  48.2 1.7 bitcast_dynamic-update-slice_fusion.2
  49.9 1.7 bitcast_dynamic-update-slice_fusion.1
  51.6 1.7 bitcast_dynamic-update-slice_fusion
  53.3 0.7 constant_dynamic-update-slice_fusion
  54.0 1.6 copy.55
  55.6 1.2 reshape.208
  56.8 1.0 bitcast_dynamic-update-slice_fusion.6
  57.8 1.0 bitcast_dynamic-update-slice_fusion.5
  58.8 1.2 reshape.206
  60.1 0.5 copy-done
  60.6 3.1 %exponential_reduce_fusion = f32[4,256]{1,0:T(4,128)S(1)} fusion(bf16[256,4,128]{2,0,1:T(8,128)(2,1)} %pad_maximum_fusion.2, pred[256,1280]{1,0:T(8,128)(4,1)S(1)} %compare_and_fusion, bf16[1280,4,128]{2,1,0:T(4,128)(2,1)S(1)} %copy-done), kind=kOutput, calls=%fused_computation.4 | convolution fusion | flops 340788480 | bytes 1904640 | tf_op jit(solution)/shard_map/sub | solution.py:61
  63.7 4.5 %fusion.6 = bf16[4,128,256]{2,1,0:T(8,128)(2,1)} fusion(f32[4,256]{1,0:T(4,128)S(1)} %exponential_reduce_fusion, bf16[1280,4,128]{2,1,0:T(4,128)(2,1)S(1)} %copy-done.1, bf16[256,4,128]{2,0,1:T(8,128)(2,1)} %pad_maximum_fusion.2, pred[256,1280]{1,0:T(8,128)(4,1)S(1)} %compare_and_fusion, bf16[1280,4,128]{2,1,0:T(4,128)(2,1)S(1)} %copy-done), kind=kOutput, calls=%fused_computation.12 | convolution fusion | flops 677775616 | bytes 3477504 | tf_op jit(solution)/shard_map/hqk,khd->qhd/dot_general | solution.py:63
  68.2 3.1 %all_gather.13 = bf16[32,1024]{1,0:T(8,128)(2,1)S(1)} all-gather(bf16[16,1024]{1,0:T(8,128)(2,1)S(1)} %copy-done.4), channel_id=1, replica_groups=mesh['z'=16,'x'=4,'core'=2,'head'=4] {'core'}, dimensions={0}, use_global_device_ids=true | all-gather | bytes 98304 | tf_op jit(solution)/shard_map/all_gather | solution.py:92
  71.3 16.0 %all_gather.14 = bf16[128,1024]{1,0:T(8,128)(2,1)} all-gather(bf16[32,1024]{1,0:T(8,128)(2,1)S(1)} %all_gather.13), channel_id=1, replica_groups=mesh['z'=16,'x'=4,'core'=2,'head'=4] {'x'}, dimensions={0}, use_global_device_ids=true | all-gather | bytes 327680 | tf_op jit(solution)/shard_map/all_gather | solution.py:93
  88.2 0.7 convolution_convert_fusion
  88.9 0.9 copy.61
  89.7 18.8 %all-gather.3.cloned.1.call-done = bf16[256,2048]{0,1:T(8,128)(2,1)} async-done(((bf16[256,512]{0,1:T(8,128)(2,1)}), bf16[256,2048]{0,1:T(8,128)(2,1)}) %all-gather.3.cloned.1.call-update) | async-done | bytes 1048592 | tf_op jit(solution)/shard_map/all_gather | solution.py:95
  108.5 80.5 %all-gather.5.cloned.1.call-done = bf16[2048,1024]{1,0:T(8,128)(2,1)} async-done(((bf16[128,1024]{1,0:T(8,128)(2,1)}), bf16[2048,1024]{1,0:T(8,128)(2,1)}) %all-gather.5.cloned.1.call-update) | async-done | bytes 4194320 | tf_op jit(solution)/shard_map/all_gather | solution.py:94
  189.0 4.6 %fusion.5 = bf16[256,1024]{1,0:T(8,128)(2,1)} fusion(bf16[256,2048]{0,1:T(8,128)(2,1)} %all-gather.3.cloned.1.call-done, bf16[2048,1024]{1,0:T(8,128)(2,1)} %all-gather.5.cloned.1.call-done, f32[1024]{0:T(1024)S(1)} %copy-done.6), kind=kOutput, calls=%fused_computation.10 | convolution fusion | flops 1074266112 | bytes 5771264 | tf_op jit(solution)/shard_map/dot_general | solution.py:96
  (61 shorter events, 3.6 us)
Async XLA Ops:
  7.2 2.2 %copy-start.5 = (s32[64]{0:T(128)S(1)}, s32[64]{0:T(128)}, u32[]{:S(2)}) copy-start(s32[64]{0:T(128)} %param.10) | copy-start | bytes 772
  7.2 101.3 %all-gather.3.cloned.1.call-start = ((), (), s32[]{:S(2)}) async-start(), calls=%async_computation | async-start | bytes 1310720 | tf_op jit(solution)/shard_map/all_gather | solution.py:95
  10.2 14.3 %copy-start.2 = (bf16[256,512]{1,0:T(8,128)(2,1)S(1)}, bf16[256,512]{1,0:T(8,128)(2,1)}, u32[]{:S(2)}) copy-start(bf16[256,512]{1,0:T(8,128)(2,1)} %param.9) | copy-start | bytes 786436
  10.2 18.7 %copy-start.3 = (bf16[256,512]{1,0:T(8,128)(2,1)S(1)}, bf16[256,512]{1,0:T(8,128)(2,1)}, u32[]{:S(2)}) copy-start(bf16[256,512]{1,0:T(8,128)(2,1)} %param.7) | copy-start | bytes 786436
  10.7 20.5 %collective-permute-start.4 = (bf16[256,512]{0,1:T(8,128)(2,1)S(1)}, bf16[256,512]{0,1:T(8,128)(2,1)S(1)}, u32[]{:S(2)}, u32[]{:S(2)}) collective-permute-start(bf16[256,512]{0,1:T(8,128)(2,1)S(1)} %bitcast.39), channel_id=1, source_target_pairs={{0,16},{4,20},{8,24},{12,28},{16,32},{20,36},{24,40},{28,44},{32,4... | collective-permute-start | bytes 786440 | tf_op jit(solution)/shard_map/ppermute | solution.py:20
  14.7 29.1 %collective-permute-start.5 = (bf16[256,512]{0,1:T(8,128)(2,1)S(1)}, bf16[256,512]{0,1:T(8,128)(2,1)}, u32[]{:S(2)}, u32[]{:S(2)}) collective-permute-start(bf16[256,512]{0,1:T(8,128)(2,1)S(1)} %bitcast.40), channel_id=1, source_target_pairs={{0,12},{4,16},{8,20},{12,24},{16,28},{20,32},{24,36},{28,40},{32,4... | collective-permute-start | bytes 786440 | tf_op jit(solution)/shard_map/ppermute | solution.py:20
  17.7 32.2 %collective-permute-start.6 = (bf16[256,512]{0,1:T(8,128)(2,1)S(1)}, bf16[256,512]{0,1:T(8,128)(2,1)}, u32[]{:S(2)}, u32[]{:S(2)}) collective-permute-start(bf16[256,512]{0,1:T(8,128)(2,1)S(1)} %bitcast.41), channel_id=1, source_target_pairs={{0,8},{4,12},{8,16},{12,20},{16,24},{20,28},{24,32},{28,36},{32,40... | collective-permute-start | bytes 786440 | tf_op jit(solution)/shard_map/ppermute | solution.py:20
  21.0 30.5 %collective-permute-start.7 = (bf16[256,512]{0,1:T(8,128)(2,1)S(1)}, bf16[256,512]{0,1:T(8,128)(2,1)}, u32[]{:S(2)}, u32[]{:S(2)}) collective-permute-start(bf16[256,512]{0,1:T(8,128)(2,1)S(1)} %bitcast.42), channel_id=1, source_target_pairs={{0,4},{4,8},{8,12},{12,16},{16,20},{20,24},{24,28},{28,32},{32,36}... | collective-permute-start | bytes 786440 | tf_op jit(solution)/shard_map/ppermute | solution.py:20
  24.6 10.1 %collective-permute-start = (bf16[256,512]{1,0:T(8,128)(2,1)S(1)}, bf16[256,512]{1,0:T(8,128)(2,1)S(1)}, u32[]{:S(2)}, u32[]{:S(2)}) collective-permute-start(bf16[256,512]{1,0:T(8,128)(2,1)S(1)} %copy-done.2), channel_id=1, source_target_pairs={{0,16},{4,20},{8,24},{12,28},{16,32},{20,36},{24,40},{28,44},{32,4... | collective-permute-start | bytes 786440 | tf_op jit(solution)/shard_map/ppermute | solution.py:20
  31.2 22.1 %collective-permute-start.1 = (bf16[256,512]{1,0:T(8,128)(2,1)S(1)}, bf16[256,512]{1,0:T(8,128)(2,1)S(1)}, u32[]{:S(2)}, u32[]{:S(2)}) collective-permute-start(bf16[256,512]{1,0:T(8,128)(2,1)S(1)} %copy-done.2), channel_id=1, source_target_pairs={{0,12},{4,16},{8,20},{12,24},{16,28},{20,32},{24,36},{28,40},{32,4... | collective-permute-start | bytes 786440 | tf_op jit(solution)/shard_map/ppermute | solution.py:20
  34.7 22.2 %collective-permute-start.2 = (bf16[256,512]{1,0:T(8,128)(2,1)S(1)}, bf16[256,512]{1,0:T(8,128)(2,1)}, u32[]{:S(2)}, u32[]{:S(2)}) collective-permute-start(bf16[256,512]{1,0:T(8,128)(2,1)S(1)} %copy-done.2), channel_id=1, source_target_pairs={{0,8},{4,12},{8,16},{12,20},{16,24},{20,28},{24,32},{28,36},{32,40... | collective-permute-start | bytes 786440 | tf_op jit(solution)/shard_map/ppermute | solution.py:20
  43.9 13.9 %collective-permute-start.3 = (bf16[256,512]{1,0:T(8,128)(2,1)S(1)}, bf16[256,512]{1,0:T(8,128)(2,1)}, u32[]{:S(2)}, u32[]{:S(2)}) collective-permute-start(bf16[256,512]{1,0:T(8,128)(2,1)S(1)} %copy-done.2), channel_id=1, source_target_pairs={{0,4},{4,8},{8,12},{12,16},{16,20},{20,24},{24,28},{28,32},{32,36}... | collective-permute-start | bytes 786440 | tf_op jit(solution)/shard_map/ppermute | solution.py:20
  58.8 1.8 copy-start
  60.6 3.1 %copy-start.1 = (bf16[1280,4,128]{2,1,0:T(4,128)(2,1)S(1)}, bf16[1280,4,128]{2,1,0:T(4,128)(2,1)}, u32[]{:S(2)}) copy-start(bf16[1280,4,128]{2,1,0:T(4,128)(2,1)} %reshape.206) | copy-start | bytes 3932164
  63.7 4.6 %copy-start.4 = (bf16[16,1024]{1,0:T(8,128)(2,1)S(1)}, bf16[16,1024]{1,0:T(8,128)(2,1)}, u32[]{:S(2)}) copy-start(bf16[16,1024]{1,0:T(8,128)(2,1)} %param.12) | copy-start | bytes 98308
  68.2 20.0 %copy-start.7 = (s32[2]{0:T(128)S(1)}, s32[2]{0:T(128)}, u32[]{:S(2)}) copy-start(s32[2]{0:T(128)} %param.11) | copy-start | bytes 28
  68.2 120.8 %all-gather.5.cloned.1.call-start = ((), (), s32[]{:S(2)}) async-start(), calls=%async_computation.1 | async-start | bytes 4456448 | tf_op jit(solution)/shard_map/all_gather | solution.py:94
  88.2 100.9 %copy-start.6 = (f32[1024]{0:T(1024)S(1)}, f32[1024]{0:T(1024)}, u32[]{:S(2)}) copy-start(f32[1024]{0:T(1024)} %param.13) | copy-start | bytes 12292
Sparse Core Ops, SparseCore 0:
  68.3 40.1 all-gather.2
  110.6 78.3 all-gather.4
where the time goes:
time: 201 us; the launch traced here: 200 us
  waiting for transfers between devices  100 us (50%)
  starting transfers between devices  34 us (17%)
  blocking collectives  19.1 us (10%)
  local copies, waits for them, and re-layouts  17.7 us (9%)
  between operations  14.5 us (7%)
  matrix products  12.8 us (6%)
  other arithmetic  2.33 us (1%)
    all_gather x1, waiting for transfers between devices, local(): weight_rows = lax.all_gather(weight_rows, 'z', axis=0, tiled=True)  80.5 us
    ppermute x8, starting transfers between devices, passed_along(): return lax.ppermute(array, axis, pairs)  33.9 us
    all_gather x1, waiting for transfers between devices, local(): heads_all = lax.all_gather(heads_out, 'head', axis=1, tiled=True)  18.8 us
    all_gather x1, blocking collectives, local(): weight_rows = lax.all_gather(weight_rows, 'x', axis=0, tiled=True)  16 us
    unnamed x29, local copies, waits for them, and re-layouts  10.7 us
    dot_general x1, matrix products, local(): summed = jnp.dot(heads_all, weight_rows, preferred_element_type=jnp.float32)  4.59 us
    dot_general x1, matrix products, attend_block(): jnp.einsum('hqk,khd->qhd', probs, value_rows, preferred_element_type=jnp....  4.48 us
  transfers between devices with their start and end apart: 10, of which 3 were waited for; matrix products, arithmetic and copies ran while one was open for 7% of the time, Pallas kernels for 0%

commit v1 on v0

--- a/solution.py
+++ b/solution.py
@@ -12,6 +12,12 @@
 TOK_DEV = 256
 rope_base = 10000.0
 REQ = ("z", "x", "core")
+
+
+def joined_along(blocks, dim):
+    blocks = jnp.moveaxis(blocks, 0, dim)
+    lengths = blocks.shape
+    return blocks.reshape(*lengths[:dim], lengths[dim] * lengths[dim + 1], *lengths[dim + 2 :])
 
 
 def passed_along(array, axis, by):
@@ -92,7 +98,19 @@
     weight_rows = lax.all_gather(out_weight, "core", axis=0, tiled=True)
     weight_rows = lax.all_gather(weight_rows, "x", axis=0, tiled=True)
     weight_rows = lax.all_gather(weight_rows, "z", axis=0, tiled=True)
-    heads_all = lax.all_gather(heads_out, "head", axis=1, tiled=True)
+    devices_2 = lax.axis_size("head")
+    pairs_2 = [(i_2, (i_2 + 1) % devices_2) for i_2 in range(devices_2)]
+    back = [(b, a) for a, b in pairs_2]
+    lower, upper = ([], [])
+    for step in range(devices_2 - 1):
+        if step % 2 == 0:
+            lower.append(lax.ppermute(lower[-1] if lower else heads_out, "head", pairs_2))
+        else:
+            upper.append(lax.ppermute(upper[-1] if upper else heads_out, "head", back))
+    tiles = jnp.stack([*lower[::-1], heads_out, *upper])
+    shift = lax.axis_index("head") - len(lower)
+    tiles = tiles[(jnp.arange(devices_2) - shift) % devices_2]
+    heads_all = joined_along(tiles, 1)
     summed = jnp.dot(heads_all, weight_rows, preferred_element_type=jnp.float32)
     attended = (summed + out_bias).astype(jnp.bfloat16)
     local_page = page_table - device_rank * BLK_DEV

time: 201 us -> 152 us (0.76)
  the two profiles are of different devices: /device:TPU:2 before, /device:TPU:256 now
where the time goes in v1:
time: 152 us; the launch traced here: 151 us
  starting transfers between devices  53.6 us (35%)
  waiting for transfers between devices  33.7 us (22%)
  local copies, waits for them, and re-layouts  18.4 us (12%)
  blocking collectives  15.5 us (10%)
  between operations  14.5 us (10%)
  matrix products  12.5 us (8%)
  other arithmetic  3.15 us (2%)
    ppermute x8, starting transfers between devices, passed_along(): return lax.ppermute(array, axis, pairs)  44.4 us
    ppermute x8, waiting for transfers between devices, passed_along(): return lax.ppermute(array, axis, pairs)  23 us
    all_gather x1, blocking collectives, local(): weight_rows = lax.all_gather(weight_rows, 'x', axis=0, tiled=True)  13.3 us
    unnamed x29, local copies, waits for them, and re-layouts  10.8 us
    ppermute x2, waiting for transfers between devices, local(): lax.ppermute(lower[-1] if lower else heads_out, 'head', pairs_2)  10.6 us
    ppermute x2, starting transfers between devices, local(): lax.ppermute(lower[-1] if lower else heads_out, 'head', pairs_2)  5.61 us
    dot_general x1, matrix products, attend_block(): jnp.einsum('hqk,khd->qhd', probs, value_rows, preferred_element_type=jnp....  4.48 us
    dot_general x1, matrix products, local(): summed = jnp.dot(heads_all, weight_rows, preferred_element_type=jnp.float32)  4.26 us
  transfers between devices with their start and end apart: 12, of which 4 were waited for; matrix products, arithmetic and copies ran while one was open for 19% of the time, Pallas kernels for 0%

profile of v1, /device:TPU:256, one launch (start us, length us, event | category | flops | bytes accessed | tf_op | source)
XLA Modules:
  0.0 151.4 jit_solution(139351428593524942)
XLA Ops:
  7.2 2.2 %all_gather.9 = bf16[32,1024]{1,0:T(8,128)(2,1)S(1)} all-gather(bf16[16,1024]{1,0:T(8,128)(2,1)} %param.12), channel_id=1, replica_groups=mesh['z'=16,'x'=4,'core'=2,'head'=4] {'core'}, dimensions={0}, use_global_device_ids=true | all-gather | bytes 98304 | tf_op jit(solution)/shard_map/all_gather | solution.py:98
  9.4 13.3 %all_gather.10 = bf16[128,1024]{1,0:T(8,128)(2,1)} all-gather(bf16[32,1024]{1,0:T(8,128)(2,1)S(1)} %all_gather.9), channel_id=1, replica_groups=mesh['z'=16,'x'=4,'core'=2,'head'=4] {'x'}, dimensions={0}, use_global_device_ids=true | all-gather | bytes 327680 | tf_op jit(solution)/shard_map/all_gather | solution.py:99
  22.8 0.7 copy.44
  25.9 3.4 %collective-permute-start.4 = (bf16[256,512]{0,1:T(8,128)(2,1)S(1)}, bf16[256,512]{0,1:T(8,128)(2,1)S(1)}, u32[]{:S(2)}, u32[]{:S(2)}) collective-permute-start(bf16[256,512]{0,1:T(8,128)(2,1)S(1)} %bitcast.49), channel_id=1, source_target_pairs={{0,16},{4,20},{8,24},{12,28},{16,32},{20,36},{24,40},{28,44},{32,4... | collective-permute-start | bytes 786440 | tf_op jit(solution)/shard_map/ppermute | solution.py:26
  29.3 1.9 %collective-permute-start.5 = (bf16[256,512]{0,1:T(8,128)(2,1)S(1)}, bf16[256,512]{0,1:T(8,128)(2,1)}, u32[]{:S(2)}, u32[]{:S(2)}) collective-permute-start(bf16[256,512]{0,1:T(8,128)(2,1)S(1)} %bitcast.50), channel_id=1, source_target_pairs={{0,12},{4,16},{8,20},{12,24},{16,28},{20,32},{24,36},{28,40},{32,4... | collective-permute-start | bytes 786440 | tf_op jit(solution)/shard_map/ppermute | solution.py:26
  31.2 3.8 %collective-permute-start.6 = (bf16[256,512]{0,1:T(8,128)(2,1)S(1)}, bf16[256,512]{0,1:T(8,128)(2,1)}, u32[]{:S(2)}, u32[]{:S(2)}) collective-permute-start(bf16[256,512]{0,1:T(8,128)(2,1)S(1)} %bitcast.51), channel_id=1, source_target_pairs={{0,8},{4,12},{8,16},{12,20},{16,24},{20,28},{24,32},{28,36},{32,40... | collective-permute-start | bytes 786440 | tf_op jit(solution)/shard_map/ppermute | solution.py:26
  35.1 3.7 %collective-permute-start.7 = (bf16[256,512]{0,1:T(8,128)(2,1)S(1)}, bf16[256,512]{0,1:T(8,128)(2,1)}, u32[]{:S(2)}, u32[]{:S(2)}) collective-permute-start(bf16[256,512]{0,1:T(8,128)(2,1)S(1)} %bitcast.52), channel_id=1, source_target_pairs={{0,4},{4,8},{8,12},{12,16},{16,20},{20,24},{24,28},{28,32},{32,36}... | collective-permute-start | bytes 786440 | tf_op jit(solution)/shard_map/ppermute | solution.py:26
  38.7 4.6 %collective-permute-start = (bf16[256,512]{1,0:T(8,128)(2,1)S(1)}, bf16[256,512]{1,0:T(8,128)(2,1)}, u32[]{:S(2)}, u32[]{:S(2)}) collective-permute-start(bf16[256,512]{1,0:T(8,128)(2,1)S(1)} %copy-done.2), channel_id=1, source_target_pairs={{0,16},{4,20},{8,24},{12,28},{16,32},{20,36},{24,40},{28,44},{32,4... | collective-permute-start | bytes 786440 | tf_op jit(solution)/shard_map/ppermute | solution.py:26
  44.6 1.0 pad_maximum_fusion.3
  45.6 1.9 %collective-permute-start.1 = (bf16[256,512]{1,0:T(8,128)(2,1)S(1)}, bf16[256,512]{1,0:T(8,128)(2,1)S(1)}, u32[]{:S(2)}, u32[]{:S(2)}) collective-permute-start(bf16[256,512]{1,0:T(8,128)(2,1)S(1)} %copy-done.2), channel_id=1, source_target_pairs={{0,12},{4,16},{8,20},{12,24},{16,28},{20,32},{24,36},{28,40},{32,4... | collective-permute-start | bytes 786440 | tf_op jit(solution)/shard_map/ppermute | solution.py:26
  48.2 10.3 %collective-permute-done = bf16[256,512]{1,0:T(8,128)(2,1)} collective-permute-done((bf16[256,512]{1,0:T(8,128)(2,1)S(1)}, bf16[256,512]{1,0:T(8,128)(2,1)}, u32[]{:S(2)}, u32[]{:S(2)}) %collective-permute-start) | collective-permute-done | bytes 262176 | tf_op jit(solution)/shard_map/ppermute | solution.py:26
  58.5 10.1 %collective-permute-start.2 = (bf16[256,512]{1,0:T(8,128)(2,1)S(1)}, bf16[256,512]{1,0:T(8,128)(2,1)}, u32[]{:S(2)}, u32[]{:S(2)}) collective-permute-start(bf16[256,512]{1,0:T(8,128)(2,1)S(1)} %copy-done.2), channel_id=1, source_target_pairs={{0,8},{4,12},{8,16},{12,20},{16,24},{20,28},{24,32},{28,36},{32,40... | collective-permute-start | bytes 786440 | tf_op jit(solution)/shard_map/ppermute | solution.py:26
  68.6 1.0 bitcast_dynamic-update-slice_fusion.8
  69.6 15.1 %collective-permute-start.3 = (bf16[256,512]{1,0:T(8,128)(2,1)S(1)}, bf16[256,512]{1,0:T(8,128)(2,1)}, u32[]{:S(2)}, u32[]{:S(2)}) collective-permute-start(bf16[256,512]{1,0:T(8,128)(2,1)S(1)} %copy-done.2), channel_id=1, source_target_pairs={{0,4},{4,8},{8,12},{12,16},{16,20},{20,24},{24,28},{28,32},{32,36}... | collective-permute-start | bytes 786440 | tf_op jit(solution)/shard_map/ppermute | solution.py:26
  84.7 1.7 %bitcast_dynamic-update-slice_fusion.2 = bf16[5,256,512]{1,2,0:T(8,128)(2,1)} fusion(bf16[5,256,512]{1,2,0:T(8,128)(2,1)} %bitcast_dynamic-update-slice_fusion.3, bf16[256,512]{0,1:T(8,128)(2,1)} %collective-permute-done.5), kind=kLoop, calls=%fused_computation.26 | loop fusion | bytes 524288
  86.4 1.7 %bitcast_dynamic-update-slice_fusion.1 = bf16[5,256,512]{1,2,0:T(8,128)(2,1)} fusion(bf16[5,256,512]{1,2,0:T(8,128)(2,1)} %bitcast_dynamic-update-slice_fusion.2, bf16[256,512]{0,1:T(8,128)(2,1)} %collective-permute-done.6), kind=kLoop, calls=%fused_computation.25 | loop fusion | bytes 524288
  88.0 1.7 %bitcast_dynamic-update-slice_fusion = bf16[5,256,512]{1,2,0:T(8,128)(2,1)} fusion(bf16[5,256,512]{1,2,0:T(8,128)(2,1)} %bitcast_dynamic-update-slice_fusion.1, bf16[256,512]{0,1:T(8,128)(2,1)} %collective-permute-done.7), kind=kLoop, calls=%fused_computation.24 | loop fusion | bytes 524288
  90.4 1.6 %copy.55 = bf16[5,256,512]{2,1,0:T(8,128)(2,1)S(1)} copy(bf16[5,256,512]{1,2,0:T(8,128)(2,1)} %constant_dynamic-update-slice_fusion) | data formatting | bytes 2621440 | tf_op jit(solution)/shard_map/stack | solution.py:89
  92.1 1.2 reshape.260
  93.3 1.0 bitcast_dynamic-update-slice_fusion.6
  94.3 12.7 %collective-permute-done.3 = bf16[256,512]{1,0:T(8,128)(2,1)} collective-permute-done((bf16[256,512]{1,0:T(8,128)(2,1)S(1)}, bf16[256,512]{1,0:T(8,128)(2,1)}, u32[]{:S(2)}, u32[]{:S(2)}) %collective-permute-start.3) | collective-permute-done | bytes 262176 | tf_op jit(solution)/shard_map/ppermute | solution.py:26
  107.0 1.0 bitcast_dynamic-update-slice_fusion.5
  108.0 1.3 reshape.258
  109.7 3.1 %exponential_reduce_fusion = f32[4,256]{1,0:T(4,128)S(1)} fusion(bf16[256,4,128]{2,0,1:T(8,128)(2,1)} %pad_maximum_fusion.3, pred[256,1280]{1,0:T(8,128)(4,1)S(1)} %compare_and_fusion, bf16[1280,4,128]{2,1,0:T(4,128)(2,1)S(1)} %copy-done), kind=kOutput, calls=%fused_computation.5 | convolution fusion | flops 340788480 | bytes 1904640 | tf_op jit(solution)/shard_map/sub | solution.py:67
  112.8 4.5 %fusion.6 = bf16[4,128,256]{2,1,0:T(8,128)(2,1)} fusion(f32[4,256]{1,0:T(4,128)S(1)} %exponential_reduce_fusion, bf16[1280,4,128]{2,1,0:T(4,128)(2,1)S(1)} %copy-done.1, bf16[256,4,128]{2,0,1:T(8,128)(2,1)} %pad_maximum_fusion.3, pred[256,1280]{1,0:T(8,128)(4,1)S(1)} %compare_and_fusion, bf16[1280,4,128]{2,1,0:T(4,128)(2,1)S(1)} %copy-done), kind=kOutput, calls=%fused_computation.13 | convolution fusion | flops 677775616 | bytes 3477504 | tf_op jit(solution)/shard_map/hqk,khd->qhd/dot_general | solution.py:69
  117.3 3.7 %collective-permute-start.8 = (bf16[256,512]{0,1:T(8,128)(2,1)}, bf16[256,512]{0,1:T(8,128)(2,1)S(1)}, u32[]{:S(2)}, u32[]{:S(2)}) collective-permute-start(bf16[256,512]{0,1:T(8,128)(2,1)} %bitcast.59), channel_id=1, source_target_pairs={{0,1},{1,2},{2,3},{3,0},{4,5},{5,6},{6,7},{7,4},{8,9},{9,10},{10,1... | collective-permute-start | bytes 786440 | tf_op jit(solution)/shard_map/ppermute | solution.py:107
  121.8 3.5 %collective-permute-start.10 = (bf16[256,512]{0,1:T(8,128)(2,1)S(1)}, bf16[256,512]{0,1:T(8,128)(2,1)S(1)}, u32[]{:S(2)}, u32[]{:S(2)}) collective-permute-start(bf16[256,512]{0,1:T(8,128)(2,1)S(1)} %bitcast.60), channel_id=1, source_target_pairs={{1,0},{2,1},{3,2},{0,3},{5,4},{6,5},{7,6},{4,7},{9,8},{10,9},{11,1... | collective-permute-start | bytes 786440 | tf_op jit(solution)/shard_map/ppermute | solution.py:109
  125.3 4.6 %collective-permute-done.8 = bf16[256,512]{0,1:T(8,128)(2,1)S(1)} collective-permute-done((bf16[256,512]{0,1:T(8,128)(2,1)}, bf16[256,512]{0,1:T(8,128)(2,1)S(1)}, u32[]{:S(2)}, u32[]{:S(2)}) %collective-permute-start.8) | collective-permute-done | bytes 262176 | tf_op jit(solution)/shard_map/ppermute | solution.py:107
  130.0 1.9 %collective-permute-start.9 = (bf16[256,512]{0,1:T(8,128)(2,1)S(1)}, bf16[256,512]{0,1:T(8,128)(2,1)S(1)}, u32[]{:S(2)}, u32[]{:S(2)}) collective-permute-start(bf16[256,512]{0,1:T(8,128)(2,1)S(1)} %collective-permute-done.8), channel_id=1, source_target_pairs={{0,1},{1,2},{2,3},{3,0},{4,5},{5,6},{6,7},{7,4},{8,9},{9,10},{10,1... | collective-permute-start | bytes 786440 | tf_op jit(solution)/shard_map/ppermute | solution.py:107
  132.6 0.9 copy.61
  133.5 6.0 %collective-permute-done.9 = bf16[256,512]{0,1:T(8,128)(2,1)S(1)} collective-permute-done((bf16[256,512]{0,1:T(8,128)(2,1)S(1)}, bf16[256,512]{0,1:T(8,128)(2,1)S(1)}, u32[]{:S(2)}, u32[]{:S(2)}) %collective-permute-start.9) | collective-permute-done | bytes 262176 | tf_op jit(solution)/shard_map/ppermute | solution.py:107
  140.3 4.3 %fusion.5 = bf16[256,1024]{1,0:T(8,128)(2,1)} fusion(bf16[256,2048]{0,1:T(8,128)(2,1)S(1)} %bitcast.56, bf16[2048,1024]{1,0:T(8,128)(2,1)} %all-gather.2.cloned.1.call-done, f32[1024]{0:T(1024)S(1)} %copy-done.6), kind=kOutput, calls=%fused_computation.11 | convolution fusion | flops 1074266112 | bytes 5771264 | tf_op jit(solution)/shard_map/dot_general | solution.py:114
  (68 shorter events, 7.8 us)
Async XLA Ops:
  7.2 17.7 %copy-start.3 = (bf16[256,512]{1,0:T(8,128)(2,1)S(1)}, bf16[256,512]{1,0:T(8,128)(2,1)}, u32[]{:S(2)}) copy-start(bf16[256,512]{1,0:T(8,128)(2,1)} %param.8) | copy-start | bytes 786436
  7.2 133.1 %all-gather.2.cloned.1.call-start = ((), (), s32[]{:S(2)}) async-start(), calls=%async_computation | async-start | bytes 4456448 | tf_op jit(solution)/shard_map/all_gather | solution.py:100
  25.5 13.3 %copy-start.2 = (bf16[256,512]{1,0:T(8,128)(2,1)S(1)}, bf16[256,512]{1,0:T(8,128)(2,1)}, u32[]{:S(2)}) copy-start(bf16[256,512]{1,0:T(8,128)(2,1)} %param.9) | copy-start | bytes 786436
  25.5 17.8 %copy-start.4 = (bf16[256,512]{1,0:T(8,128)(2,1)S(1)}, bf16[256,512]{1,0:T(8,128)(2,1)}, u32[]{:S(2)}) copy-start(bf16[256,512]{1,0:T(8,128)(2,1)} %param.7) | copy-start | bytes 786436
  25.9 19.6 %collective-permute-start.4 = (bf16[256,512]{0,1:T(8,128)(2,1)S(1)}, bf16[256,512]{0,1:T(8,128)(2,1)S(1)}, u32[]{:S(2)}, u32[]{:S(2)}) collective-permute-start(bf16[256,512]{0,1:T(8,128)(2,1)S(1)} %bitcast.49), channel_id=1, source_target_pairs={{0,16},{4,20},{8,24},{12,28},{16,32},{20,36},{24,40},{28,44},{32,4... | collective-permute-start | bytes 786440 | tf_op jit(solution)/shard_map/ppermute | solution.py:26
  29.3 40.3 %collective-permute-start.5 = (bf16[256,512]{0,1:T(8,128)(2,1)S(1)}, bf16[256,512]{0,1:T(8,128)(2,1)}, u32[]{:S(2)}, u32[]{:S(2)}) collective-permute-start(bf16[256,512]{0,1:T(8,128)(2,1)S(1)} %bitcast.50), channel_id=1, source_target_pairs={{0,12},{4,16},{8,20},{12,24},{16,28},{20,32},{24,36},{28,40},{32,4... | collective-permute-start | bytes 786440 | tf_op jit(solution)/shard_map/ppermute | solution.py:26
  31.2 55.1 %collective-permute-start.6 = (bf16[256,512]{0,1:T(8,128)(2,1)S(1)}, bf16[256,512]{0,1:T(8,128)(2,1)}, u32[]{:S(2)}, u32[]{:S(2)}) collective-permute-start(bf16[256,512]{0,1:T(8,128)(2,1)S(1)} %bitcast.51), channel_id=1, source_target_pairs={{0,8},{4,12},{8,16},{12,20},{16,24},{20,28},{24,32},{28,36},{32,40... | collective-permute-start | bytes 786440 | tf_op jit(solution)/shard_map/ppermute | solution.py:26
  35.1 53.0 %collective-permute-start.7 = (bf16[256,512]{0,1:T(8,128)(2,1)S(1)}, bf16[256,512]{0,1:T(8,128)(2,1)}, u32[]{:S(2)}, u32[]{:S(2)}) collective-permute-start(bf16[256,512]{0,1:T(8,128)(2,1)S(1)} %bitcast.52), channel_id=1, source_target_pairs={{0,4},{4,8},{8,12},{12,16},{16,20},{20,24},{24,28},{28,32},{32,36}... | collective-permute-start | bytes 786440 | tf_op jit(solution)/shard_map/ppermute | solution.py:26
  38.7 19.8 %collective-permute-start = (bf16[256,512]{1,0:T(8,128)(2,1)S(1)}, bf16[256,512]{1,0:T(8,128)(2,1)}, u32[]{:S(2)}, u32[]{:S(2)}) collective-permute-start(bf16[256,512]{1,0:T(8,128)(2,1)S(1)} %copy-done.2), channel_id=1, source_target_pairs={{0,16},{4,20},{8,24},{12,28},{16,32},{20,36},{24,40},{28,44},{32,4... | collective-permute-start | bytes 786440 | tf_op jit(solution)/shard_map/ppermute | solution.py:26
  45.6 44.2 %collective-permute-start.1 = (bf16[256,512]{1,0:T(8,128)(2,1)S(1)}, bf16[256,512]{1,0:T(8,128)(2,1)S(1)}, u32[]{:S(2)}, u32[]{:S(2)}) collective-permute-start(bf16[256,512]{1,0:T(8,128)(2,1)S(1)} %copy-done.2), channel_id=1, source_target_pairs={{0,12},{4,16},{8,20},{12,24},{16,28},{20,32},{24,36},{28,40},{32,4... | collective-permute-start | bytes 786440 | tf_op jit(solution)/shard_map/ppermute | solution.py:26
  58.5 34.8 %collective-permute-start.2 = (bf16[256,512]{1,0:T(8,128)(2,1)S(1)}, bf16[256,512]{1,0:T(8,128)(2,1)}, u32[]{:S(2)}, u32[]{:S(2)}) collective-permute-start(bf16[256,512]{1,0:T(8,128)(2,1)S(1)} %copy-done.2), channel_id=1, source_target_pairs={{0,8},{4,12},{8,16},{12,20},{16,24},{20,28},{24,32},{28,36},{32,40... | collective-permute-start | bytes 786440 | tf_op jit(solution)/shard_map/ppermute | solution.py:26
  69.6 37.4 %collective-permute-start.3 = (bf16[256,512]{1,0:T(8,128)(2,1)S(1)}, bf16[256,512]{1,0:T(8,128)(2,1)}, u32[]{:S(2)}, u32[]{:S(2)}) collective-permute-start(bf16[256,512]{1,0:T(8,128)(2,1)S(1)} %copy-done.2), channel_id=1, source_target_pairs={{0,4},{4,8},{8,12},{12,16},{16,20},{20,24},{24,28},{28,32},{32,36}... | collective-permute-start | bytes 786440 | tf_op jit(solution)/shard_map/ppermute | solution.py:26
  108.0 1.8 %copy-start = (bf16[1280,4,128]{2,1,0:T(4,128)(2,1)S(1)}, bf16[1280,4,128]{2,1,0:T(4,128)(2,1)}, u32[]{:S(2)}) copy-start(bf16[1280,4,128]{2,1,0:T(4,128)(2,1)} %reshape.260) | copy-start | bytes 3932164
  109.7 3.1 %copy-start.1 = (bf16[1280,4,128]{2,1,0:T(4,128)(2,1)S(1)}, bf16[1280,4,128]{2,1,0:T(4,128)(2,1)}, u32[]{:S(2)}) copy-start(bf16[1280,4,128]{2,1,0:T(4,128)(2,1)} %reshape.258) | copy-start | bytes 3932164
  117.3 4.5 %copy-start.7 = (s32[2]{0:T(128)S(1)}, s32[2]{0:T(128)}, u32[]{:S(2)}) copy-start(s32[2]{0:T(128)} %param.11) | copy-start | bytes 28
  117.3 4.5 %copy-start.5 = (bf16[4,128,256]{2,1,0:T(8,128)(2,1)S(1)}, bf16[4,128,256]{2,1,0:T(8,128)(2,1)}, u32[]{:S(2)}) copy-start(bf16[4,128,256]{2,1,0:T(8,128)(2,1)} %fusion.6) | copy-start | bytes 786436
  117.3 12.7 %collective-permute-start.8 = (bf16[256,512]{0,1:T(8,128)(2,1)}, bf16[256,512]{0,1:T(8,128)(2,1)S(1)}, u32[]{:S(2)}, u32[]{:S(2)}) collective-permute-start(bf16[256,512]{0,1:T(8,128)(2,1)} %bitcast.59), channel_id=1, source_target_pairs={{0,1},{1,2},{2,3},{3,0},{4,5},{5,6},{6,7},{7,4},{8,9},{9,10},{10,1... | collective-permute-start | bytes 786440 | tf_op jit(solution)/shard_map/ppermute | solution.py:107
  121.8 11.7 %collective-permute-start.10 = (bf16[256,512]{0,1:T(8,128)(2,1)S(1)}, bf16[256,512]{0,1:T(8,128)(2,1)S(1)}, u32[]{:S(2)}, u32[]{:S(2)}) collective-permute-start(bf16[256,512]{0,1:T(8,128)(2,1)S(1)} %bitcast.60), channel_id=1, source_target_pairs={{1,0},{2,1},{3,2},{0,3},{5,4},{6,5},{7,6},{4,7},{9,8},{10,9},{11,1... | collective-permute-start | bytes 786440 | tf_op jit(solution)/shard_map/ppermute | solution.py:109
  130.0 9.5 %collective-permute-start.9 = (bf16[256,512]{0,1:T(8,128)(2,1)S(1)}, bf16[256,512]{0,1:T(8,128)(2,1)S(1)}, u32[]{:S(2)}, u32[]{:S(2)}) collective-permute-start(bf16[256,512]{0,1:T(8,128)(2,1)S(1)} %collective-permute-done.8), channel_id=1, source_target_pairs={{0,1},{1,2},{2,3},{3,0},{4,5},{5,6},{6,7},{7,4},{8,9},{9,10},{10,1... | collective-permute-start | bytes 786440 | tf_op jit(solution)/shard_map/ppermute | solution.py:107
  139.6 0.7 copy-start.6
Sparse Core Ops, SparseCore 0:
  22.9 73.9 all-gather.1
